TPU v7x, 32 devices: a whole 2x2x4 slice. The times are simulated.
32 devices in a mesh: section: 2 (over core), row: 4 (over y, x), col: 4 (over z).
Axes of the slice: x: 2, y: 2, z: 4, core: 2. Of those that a mesh axis runs over, the one named last changes fastest.
Arguments:
- checkpoints: bfloat16 [2, 4, 64, 128, 128], P('section', None, 'row', 'col'), may hold values from -1 to 1
- kernels: bfloat16 [4, 3, 3, 128, 128], P('section'), may hold values from -0.25 to 0.25
- cotangent: bfloat16 [4, 64, 128, 128], P(None, 'row', 'col'), may hold values from -1.5 to 1.5
- plan: int32 [4], replicated, may hold values from 0 to 3, each once
Outputs:
- boundary_grad: bfloat16 [2, 4, 64, 128, 128], P('section', None, 'row', 'col')
- kernel_grad: float32 [4, 3, 3, 128, 128], P('section')
Inputs may be any that keep to these rules, and one draw needn't show every extreme that they name: plan names each of the 4 microbatches exactly once; slot k of cotangent belongs to microbatch plan[k].
All inputs are finite; a program needn't handle non-finite values.
Results may differ from a plain program's by a relative error of at most 0.015.
Values may be sent and summed in bfloat16 or wider, within the bound.
No kernel may reach another device: no remote copies, remote signals or barrier semaphores. Data moves between devices by JAX's collectives and lax.ppermute only.
A program may use at most 64 MiB of HBM per device.

v0:
```python
import jax
import jax.numpy as jnp
from jax import lax
from jax.sharding import PartitionSpec as P


def extended(block, sides, width):
    for axis, dim in sides:
        count = lax.axis_size(axis)
        forward = [(i, i + 1) for i in range(count - 1)]
        backward = [(target, source) for source, target in forward]
        low = lax.ppermute(
            lax.slice_in_dim(block, block.shape[dim] - width, None, axis=dim), axis, forward
        )
        high = lax.ppermute(lax.slice_in_dim(block, 0, width, axis=dim), axis, backward)
        block = jnp.concatenate([low, block, high], axis=dim)
    return block


def passed_along(block, axis, distance):
    devices = range(lax.axis_size(axis))
    route = [(i - distance, i) for i in devices if i - distance in devices]
    return lax.ppermute(block, axis, route)


def convolve(padded, kernel):
    return lax.conv_general_dilated(
        padded,
        kernel,
        (1, 1),
        "VALID",
        dimension_numbers=("NHWC", "HWIO", "NHWC"),
        preferred_element_type=jnp.float32,
    )


def take_slots(values_in, slot_first, group_size):
    return lax.dynamic_slice_in_dim(values_in, slot_first, group_size, 0)


def kernel_terms(padded, signal):
    channels = signal.shape[3]
    flat_signal = signal.reshape(-1, channels)
    rows_out = []
    for a in range(3):
        tap_row = []
        for b in range(3):
            window = padded[:, a : a + signal.shape[1], b : b + signal.shape[2]].reshape(
                -1, channels
            )
            tap_row.append(
                lax.dot_general(
                    window,
                    flat_signal,
                    (((0,), (0,)), ((), ())),
                    preferred_element_type=jnp.float32,
                )
            )
        rows_out.append(jnp.stack(tap_row))
    return jnp.stack(rows_out)


def local(checkpoints, kernels, cotangent, plan):
    sections_count = lax.axis_size("section")
    section_index = lax.axis_index("section")
    batches = checkpoints.shape[1]
    tile_rows = checkpoints.shape[2]
    tile_cols = checkpoints.shape[3]
    channels = checkpoints.shape[4]
    layer_count = kernels.shape[0]
    flipped = jnp.transpose(kernels[:, ::-1, ::-1], (0, 1, 2, 4, 3))
    first_input = jnp.take(checkpoints[0], plan, axis=0)
    inputs_list = []
    outputs_list = []
    input_margin = []
    output_margin = []
    current = first_input
    for layer_idx in range(layer_count):
        padded = extended(current, (("row", 1), ("col", 2)), 1)
        inputs_list.append(padded)
        input_margin.append(1)
        current = jnp.tanh(convolve(padded, kernels[layer_idx])).astype(jnp.bfloat16)
        outputs_list.append(current)
        output_margin.append(0)
    groups = batches // batches
    tick_count = groups + sections_count - 1

    def backward(top_grad, slot_first):
        signals = [None] * layer_count
        gradient = top_grad.astype(jnp.float32)
        for layer_idx in reversed(range(layer_count)):
            output = take_slots(outputs_list[layer_idx], slot_first, batches).astype(jnp.float32)
            signal = (gradient * (1.0 - output * output)).astype(jnp.bfloat16)
            signals[layer_idx] = signal
            padded = extended(signal, (("row", 1), ("col", 2)), 1)
            gradient = convolve(padded, flipped[layer_idx])
        return (gradient.astype(jnp.bfloat16), signals)

    def tick_step(tick_idx, loop_state):
        incoming, boundary, gathered = loop_state
        slot_group = tick_idx - (sections_count - 1 - section_index)
        is_valid = (slot_group >= 0) & (slot_group < groups)
        slot_first = jnp.clip(slot_group, 0, groups - 1) * batches
        top_grad = jnp.where(section_index == sections_count - 1, cotangent, incoming)
        result, signals = backward(top_grad, slot_first)
        previous = boundary
        boundary = lax.dynamic_update_slice_in_dim(
            boundary, jnp.where(is_valid, result, previous), slot_first, 0
        )
        tap_terms = jnp.stack(
            [
                kernel_terms(
                    take_slots(inputs_list[layer_idx], slot_first, batches), signals[layer_idx]
                )
                for layer_idx in range(layer_count)
            ]
        )
        gathered = gathered + jnp.where(is_valid, tap_terms, 0.0)
        incoming = passed_along(result, "section", -1)
        return (incoming, boundary, gathered)

    incoming_zero = jnp.zeros((batches, tile_rows, tile_cols, channels), jnp.bfloat16)
    boundary_zero = jnp.zeros((batches, tile_rows, tile_cols, channels), jnp.bfloat16)
    gathered_zero = jnp.zeros((layer_count, 3, 3, channels, channels), jnp.float32)
    incoming, boundary, gathered = lax.fori_loop(
        0, tick_count, tick_step, (incoming_zero, boundary_zero, gathered_zero)
    )
    kernel_grad = (
        lax.psum(gathered.astype(jnp.bfloat16), ("row", "col")).astype(jnp.float32) / batches
    )
    boundary_grad = jnp.zeros_like(boundary).at[plan].set(boundary)[None]
    return (boundary_grad, kernel_grad)


def solution(mesh):
    return jax.shard_map(
        local,
        mesh=mesh,
        in_specs=(
            P("section", None, "row", "col", None),
            P("section", None, None, None, None),
            P(None, "row", "col", None),
            P(),
        ),
        out_specs=(P("section", None, "row", "col", None), P("section", None, None, None, None)),
        check_vma=False,
    )
```

profile of v0, /device:TPU:0, one launch (start us, length us, event | category | flops | bytes accessed | tf_op | source)
XLA Modules:
  0.0 291.0 jit_solution(17927654028252971086)
XLA Ops:
  10.8 5.5 %collective-permute-start.9 = (bf16[4,1,32,128]{3,2,1,0:T(8,128)(2,1)S(1)}, bf16[4,1,32,128]{3,2,1,0:T(8,128)(2,1)S(1)}, u32[]{:S(2)}, u32[]{:S(2)}) collective-permute-start(bf16[4,1,32,128]{3,2,1,0:T(8,128)(2,1)S(1)} %get-tuple-element.383), channel_id=1, source_target_pairs={{0,4},{4,8},{8,12},{1,5},{5,9},{9,13},{2,6},{6,10},{10,14},{3,7},{... | collective-permute-start | bytes 98312 | tf_op jit(solution)/shard_map/ppermute | solution.py:12
  18.5 4.0 %collective-permute-start.11 = (bf16[4,18,1,128]{3,2,1,0:T(2,128)(2,1)}, bf16[4,18,1,128]{3,2,1,0:T(2,128)(2,1)S(1)}, u32[]{:S(2)}, u32[]{:S(2)}) collective-permute-start(bf16[4,18,1,128]{3,2,1,0:T(2,128)(2,1)} %get-tuple-element.381), channel_id=1, source_target_pairs={{0,1},{1,2},{2,3},{4,5},{5,6},{6,7},{8,9},{9,10},{10,11},{12,13},{... | collective-permute-start | bytes 55304 | tf_op jit(solution)/shard_map/ppermute | solution.py:12
  26.0 2.6 collective-permute-done.12
  30.2 1.7 fusion.39
  35.1 4.9 %collective-permute-start.13 = (bf16[4,1,32,128]{3,2,0,1:T(8,128)(2,1)S(1)}, bf16[4,1,32,128]{3,2,0,1:T(8,128)(2,1)S(1)}, u32[]{:S(2)}, u32[]{:S(2)}) collective-permute-start(bf16[4,1,32,128]{3,2,0,1:T(8,128)(2,1)S(1)} %slice_bitcast_fusion.5), channel_id=1, source_target_pairs={{0,4},{4,8},{8,12},{1,5},{5,9},{9,13},{2,6},{6,10},{10,14},{3,7},{... | collective-permute-start | bytes 98312 | tf_op jit(solution)/shard_map/ppermute | solution.py:12
  41.7 3.5 %collective-permute-start.15 = (bf16[4,18,1,128]{3,1,2,0:T(8,128)(2,1)S(1)}, bf16[4,18,1,128]{3,1,2,0:T(8,128)(2,1)S(1)}, u32[]{:S(2)}, u32[]{:S(2)}) collective-permute-start(bf16[4,18,1,128]{3,1,2,0:T(8,128)(2,1)S(1)} %get-tuple-element.377), channel_id=1, source_target_pairs={{0,1},{1,2},{2,3},{4,5},{5,6},{6,7},{8,9},{9,10},{10,11},{12,13},{... | collective-permute-start | bytes 55304 | tf_op jit(solution)/shard_map/ppermute | solution.py:12
  48.0 3.0 %collective-permute-done.16 = bf16[4,18,1,128]{3,1,2,0:T(8,128)(2,1)S(1)} collective-permute-done((bf16[4,18,1,128]{3,1,2,0:T(8,128)(2,1)S(1)}, bf16[4,18,1,128]{3,1,2,0:T(8,128)(2,1)S(1)}, u32[]{:S(2)}, u32[]{:S(2)}) %collective-permute-start.16) | collective-permute-done | bytes 18464 | tf_op jit(solution)/shard_map/ppermute | solution.py:15
  50.9 1.4 pad_maximum_fusion.6
  53.9 1.7 fusion.38
  57.6 106.7 %while.20 = (s32[]{:T(128)}, bf16[4,16,32,128]{3,1,2,0:T(8,128)(2,1)}, bf16[4,16,32,128]{3,1,2,0:T(8,128)(2,1)}, f32[2,3,3,128,128]{3,4,2,1,0:T(8,128)S(1)}, pre...) while((s32[]{:T(128)}, ...), condition=%wide.region_1.2_spmd.clone, body=%wide.region_0.1_spmd.clone.sunk | while | flops 2737602560 | bytes 72510144 | solution.py:125
  57.6 1.7 multiply_convert_fusion.2
  60.7 5.8 %collective-permute-start.1 = (bf16[4,1,32,128]{3,1,2,0:T(2,128)(2,1)S(1)}, bf16[4,1,32,128]{3,1,2,0:T(2,128)(2,1)S(1)}, u32[]{:S(2)}, u32[]{:S(2)}) collective-permute-start(bf16[4,1,32,128]{3,1,2,0:T(2,128)(2,1)S(1)} %get-tuple-element.471), channel_id=1, source_target_pairs={{0,4},{4,8},{8,12},{1,5},{5,9},{9,13},{2,6},{6,10},{10,14},{3,7},{... | collective-permute-start | bytes 98312 | tf_op jit(solution)/shard_map/while/body/eval_jaxpr/ppermute | solution.py:12
  71.0 5.2 %collective-permute-start.3 = (bf16[4,18,1,128]{3,1,2,0:T(8,128)(2,1)S(1)}, bf16[4,18,1,128]{3,1,2,0:T(8,128)(2,1)}, u32[]{:S(2)}, u32[]{:S(2)}) collective-permute-start(bf16[4,18,1,128]{3,1,2,0:T(8,128)(2,1)S(1)} %get-tuple-element.473), channel_id=1, source_target_pairs={{0,1},{1,2},{2,3},{4,5},{5,6},{6,7},{8,9},{9,10},{10,11},{12,13},{... | collective-permute-start | bytes 55304 | tf_op jit(solution)/shard_map/while/body/eval_jaxpr/ppermute | solution.py:12
  79.8 1.7 convolution_select_fusion.5
  88.0 5.7 %collective-permute-start.5 = (bf16[4,1,32,128]{3,1,2,0:T(2,128)(2,1)S(1)}, bf16[4,1,32,128]{3,1,2,0:T(2,128)(2,1)S(1)}, u32[]{:S(2)}, u32[]{:S(2)}) collective-permute-start(bf16[4,1,32,128]{3,1,2,0:T(2,128)(2,1)S(1)} %get-tuple-element.475), channel_id=1, source_target_pairs={{0,4},{4,8},{8,12},{1,5},{5,9},{9,13},{2,6},{6,10},{10,14},{3,7},{... | collective-permute-start | bytes 98312 | tf_op jit(solution)/shard_map/while/body/eval_jaxpr/ppermute | solution.py:12
  94.0 1.6 collective-permute-done.5
  96.9 4.9 %collective-permute-start.7 = (bf16[4,18,1,128]{3,1,2,0:T(8,128)(2,1)S(1)}, bf16[4,18,1,128]{3,1,2,0:T(8,128)(2,1)S(1)}, u32[]{:S(2)}, u32[]{:S(2)}) collective-permute-start(bf16[4,18,1,128]{3,1,2,0:T(8,128)(2,1)S(1)} %get-tuple-element.477), channel_id=1, source_target_pairs={{0,1},{1,2},{2,3},{4,5},{5,6},{6,7},{8,9},{9,10},{10,11},{12,13},{... | collective-permute-start | bytes 55304 | tf_op jit(solution)/shard_map/while/body/eval_jaxpr/ppermute | solution.py:12
  102.0 1.4 collective-permute-done.7
  104.9 1.7 fusion.166
  109.5 1.3 collective-permute-done.8
  110.9 1.7 multiply_convert_fusion.2
  114.0 5.4 %collective-permute-start.1 = (bf16[4,1,32,128]{3,1,2,0:T(2,128)(2,1)S(1)}, bf16[4,1,32,128]{3,1,2,0:T(2,128)(2,1)S(1)}, u32[]{:S(2)}, u32[]{:S(2)}) collective-permute-start(bf16[4,1,32,128]{3,1,2,0:T(2,128)(2,1)S(1)} %get-tuple-element.471), channel_id=1, source_target_pairs={{0,4},{4,8},{8,12},{1,5},{5,9},{9,13},{2,6},{6,10},{10,14},{3,7},{... | collective-permute-start | bytes 98312 | tf_op jit(solution)/shard_map/while/body/eval_jaxpr/ppermute | solution.py:12
  124.0 5.5 %collective-permute-start.3 = (bf16[4,18,1,128]{3,1,2,0:T(8,128)(2,1)S(1)}, bf16[4,18,1,128]{3,1,2,0:T(8,128)(2,1)}, u32[]{:S(2)}, u32[]{:S(2)}) collective-permute-start(bf16[4,18,1,128]{3,1,2,0:T(8,128)(2,1)S(1)} %get-tuple-element.473), channel_id=1, source_target_pairs={{0,1},{1,2},{2,3},{4,5},{5,6},{6,7},{8,9},{9,10},{10,11},{12,13},{... | collective-permute-start | bytes 55304 | tf_op jit(solution)/shard_map/while/body/eval_jaxpr/ppermute | solution.py:12
  133.1 1.7 convolution_select_fusion.5
  141.3 5.8 %collective-permute-start.5 = (bf16[4,1,32,128]{3,1,2,0:T(2,128)(2,1)S(1)}, bf16[4,1,32,128]{3,1,2,0:T(2,128)(2,1)S(1)}, u32[]{:S(2)}, u32[]{:S(2)}) collective-permute-start(bf16[4,1,32,128]{3,1,2,0:T(2,128)(2,1)S(1)} %get-tuple-element.475), channel_id=1, source_target_pairs={{0,4},{4,8},{8,12},{1,5},{5,9},{9,13},{2,6},{6,10},{10,14},{3,7},{... | collective-permute-start | bytes 98312 | tf_op jit(solution)/shard_map/while/body/eval_jaxpr/ppermute | solution.py:12
  147.4 1.6 collective-permute-done.5
  150.3 4.9 %collective-permute-start.7 = (bf16[4,18,1,128]{3,1,2,0:T(8,128)(2,1)S(1)}, bf16[4,18,1,128]{3,1,2,0:T(8,128)(2,1)S(1)}, u32[]{:S(2)}, u32[]{:S(2)}) collective-permute-start(bf16[4,18,1,128]{3,1,2,0:T(8,128)(2,1)S(1)} %get-tuple-element.477), channel_id=1, source_target_pairs={{0,1},{1,2},{2,3},{4,5},{5,6},{6,7},{8,9},{9,10},{10,11},{12,13},{... | collective-permute-start | bytes 55304 | tf_op jit(solution)/shard_map/while/body/eval_jaxpr/ppermute | solution.py:12
  155.3 1.4 collective-permute-done.7
  158.3 1.7 fusion.166
  162.0 2.0 select_select_fusion.2
  167.4 114.6 %all-reduce.2.cloned.1.call-done = bf16[2,3,3,128,128]{4,3,2,1,0:T(8,128)(2,1)} async-done(((bf16[2,3,3,128,128]{4,3,2,1,0:T(8,128)(2,1)}), bf16[2,3,3,128,128]{4,3,2,1,0:T(8,128)(2,1)}) %all-reduce.2.cloned.1.call-update) | async-done | bytes 589840 | tf_op jit(solution)/shard_map/psum | solution.py:129
  282.0 2.2 convert_multiply_fusion
  (198 shorter events, 68.0 us)
Async XLA Ops:
  7.2 9.1 %copy-start.6 = (bf16[2,3,3,128,128]{4,3,2,1,0:T(8,128)(2,1)S(1)}, bf16[2,3,3,128,128]{4,3,2,1,0:T(8,128)(2,1)}, u32[]{:S(2)}) copy-start(bf16[2,3,3,128,128]{4,3,2,1,0:T(8,128)(2,1)} %param.7) | copy-start | bytes 1769476
  7.2 274.8 %all-reduce.2.cloned.1.call-start = ((), (), s32[]{:S(2)}) async-start(), calls=%async_computation | async-start | bytes 1179648 | tf_op jit(solution)/shard_map/psum | solution.py:129
  9.5 7.1 %collective-permute-start.10 = (bf16[4,1,32,128]{3,2,1,0:T(8,128)(2,1)S(1)}, bf16[4,1,32,128]{3,2,1,0:T(8,128)(2,1)S(1)}, u32[]{:S(2)}, u32[]{:S(2)}) collective-permute-start(bf16[4,1,32,128]{3,2,1,0:T(8,128)(2,1)S(1)} %get-tuple-element.384), channel_id=1, source_target_pairs={{4,0},{8,4},{12,8},{5,1},{9,5},{13,9},{6,2},{10,6},{14,10},{7,3},{... | collective-permute-start | bytes 98312 | tf_op jit(solution)/shard_map/ppermute | solution.py:15
  10.8 7.1 %collective-permute-start.9 = (bf16[4,1,32,128]{3,2,1,0:T(8,128)(2,1)S(1)}, bf16[4,1,32,128]{3,2,1,0:T(8,128)(2,1)S(1)}, u32[]{:S(2)}, u32[]{:S(2)}) collective-permute-start(bf16[4,1,32,128]{3,2,1,0:T(8,128)(2,1)S(1)} %get-tuple-element.383), channel_id=1, source_target_pairs={{0,4},{4,8},{8,12},{1,5},{5,9},{9,13},{2,6},{6,10},{10,14},{3,7},{... | collective-permute-start | bytes 98312 | tf_op jit(solution)/shard_map/ppermute | solution.py:12
  18.5 7.5 %collective-permute-start.11 = (bf16[4,18,1,128]{3,2,1,0:T(2,128)(2,1)}, bf16[4,18,1,128]{3,2,1,0:T(2,128)(2,1)S(1)}, u32[]{:S(2)}, u32[]{:S(2)}) collective-permute-start(bf16[4,18,1,128]{3,2,1,0:T(2,128)(2,1)} %get-tuple-element.381), channel_id=1, source_target_pairs={{0,1},{1,2},{2,3},{4,5},{5,6},{6,7},{8,9},{9,10},{10,11},{12,13},{... | collective-permute-start | bytes 55304 | tf_op jit(solution)/shard_map/ppermute | solution.py:12
  22.5 6.1 %collective-permute-start.12 = (bf16[4,18,1,128]{3,2,1,0:T(2,128)(2,1)}, bf16[4,18,1,128]{3,2,1,0:T(2,128)(2,1)S(1)}, u32[]{:S(2)}, u32[]{:S(2)}) collective-permute-start(bf16[4,18,1,128]{3,2,1,0:T(2,128)(2,1)} %get-tuple-element.382), channel_id=1, source_target_pairs={{1,0},{2,1},{3,2},{5,4},{6,5},{7,6},{9,8},{10,9},{11,10},{13,12},{... | collective-permute-start | bytes 55304 | tf_op jit(solution)/shard_map/ppermute | solution.py:15
  33.8 7.9 %collective-permute-start.14 = (bf16[4,1,32,128]{3,1,2,0:T(2,128)(2,1)}, bf16[4,1,32,128]{3,1,2,0:T(2,128)(2,1)S(1)}, u32[]{:S(2)}, u32[]{:S(2)}) collective-permute-start(bf16[4,1,32,128]{3,1,2,0:T(2,128)(2,1)} %copy.87), channel_id=1, source_target_pairs={{4,0},{8,4},{12,8},{5,1},{9,5},{13,9},{6,2},{10,6},{14,10},{7,3},{... | collective-permute-start | bytes 98312 | tf_op jit(solution)/shard_map/ppermute | solution.py:15
  35.1 6.5 %collective-permute-start.13 = (bf16[4,1,32,128]{3,2,0,1:T(8,128)(2,1)S(1)}, bf16[4,1,32,128]{3,2,0,1:T(8,128)(2,1)S(1)}, u32[]{:S(2)}, u32[]{:S(2)}) collective-permute-start(bf16[4,1,32,128]{3,2,0,1:T(8,128)(2,1)S(1)} %slice_bitcast_fusion.5), channel_id=1, source_target_pairs={{0,4},{4,8},{8,12},{1,5},{5,9},{9,13},{2,6},{6,10},{10,14},{3,7},{... | collective-permute-start | bytes 98312 | tf_op jit(solution)/shard_map/ppermute | solution.py:12
  41.7 6.2 %collective-permute-start.15 = (bf16[4,18,1,128]{3,1,2,0:T(8,128)(2,1)S(1)}, bf16[4,18,1,128]{3,1,2,0:T(8,128)(2,1)S(1)}, u32[]{:S(2)}, u32[]{:S(2)}) collective-permute-start(bf16[4,18,1,128]{3,1,2,0:T(8,128)(2,1)S(1)} %get-tuple-element.377), channel_id=1, source_target_pairs={{0,1},{1,2},{2,3},{4,5},{5,6},{6,7},{8,9},{9,10},{10,11},{12,13},{... | collective-permute-start | bytes 55304 | tf_op jit(solution)/shard_map/ppermute | solution.py:12
  45.2 5.7 %collective-permute-start.16 = (bf16[4,18,1,128]{3,1,2,0:T(8,128)(2,1)S(1)}, bf16[4,18,1,128]{3,1,2,0:T(8,128)(2,1)S(1)}, u32[]{:S(2)}, u32[]{:S(2)}) collective-permute-start(bf16[4,18,1,128]{3,1,2,0:T(8,128)(2,1)S(1)} %get-tuple-element.378), channel_id=1, source_target_pairs={{1,0},{2,1},{3,2},{5,4},{6,5},{7,6},{9,8},{10,9},{11,10},{13,12},{... | collective-permute-start | bytes 55304 | tf_op jit(solution)/shard_map/ppermute | solution.py:15
  57.6 9.2 %copy-start.1 = (bf16[4,16,32,128]{3,1,2,0:T(8,128)(2,1)}, bf16[4,16,32,128]{3,1,2,0:T(8,128)(2,1)S(1)}, u32[]{:S(2)}) copy-start(bf16[4,16,32,128]{3,1,2,0:T(8,128)(2,1)S(1)} %get-tuple-element.519) | copy-start | bytes 1572868 | tf_op jit(solution)/shard_map/while
  57.6 8.9 %copy-start.4 = (bf16[4,18,34,128]{3,1,2,0:T(8,128)(2,1)S(1)}, bf16[4,18,34,128]{3,1,2,0:T(8,128)(2,1)}, u32[]{:S(2)}) copy-start(bf16[4,18,34,128]{3,1,2,0:T(8,128)(2,1)} %get-tuple-element.525) | copy-start | bytes 1880068 | tf_op jit(solution)/shard_map/while
  59.4 10.2 %collective-permute-start = (bf16[4,1,32,128]{3,1,2,0:T(2,128)(2,1)S(1)}, bf16[4,1,32,128]{3,1,2,0:T(2,128)(2,1)S(1)}, u32[]{:S(2)}, u32[]{:S(2)}) collective-permute-start(bf16[4,1,32,128]{3,1,2,0:T(2,128)(2,1)S(1)} %get-tuple-element.470), channel_id=1, source_target_pairs={{4,0},{8,4},{12,8},{5,1},{9,5},{13,9},{6,2},{10,6},{14,10},{7,3},{... | collective-permute-start | bytes 98312 | tf_op jit(solution)/shard_map/while/body/eval_jaxpr/ppermute | solution.py:15
  60.7 8.9 %collective-permute-start.1 = (bf16[4,1,32,128]{3,1,2,0:T(2,128)(2,1)S(1)}, bf16[4,1,32,128]{3,1,2,0:T(2,128)(2,1)S(1)}, u32[]{:S(2)}, u32[]{:S(2)}) collective-permute-start(bf16[4,1,32,128]{3,1,2,0:T(2,128)(2,1)S(1)} %get-tuple-element.471), channel_id=1, source_target_pairs={{0,4},{4,8},{8,12},{1,5},{5,9},{9,13},{2,6},{6,10},{10,14},{3,7},{... | collective-permute-start | bytes 98312 | tf_op jit(solution)/shard_map/while/body/eval_jaxpr/ppermute | solution.py:12
  69.7 6.5 %collective-permute-start.2 = (bf16[4,18,1,128]{3,1,2,0:T(8,128)(2,1)S(1)}, bf16[4,18,1,128]{3,1,2,0:T(8,128)(2,1)S(1)}, u32[]{:S(2)}, u32[]{:S(2)}) collective-permute-start(bf16[4,18,1,128]{3,1,2,0:T(8,128)(2,1)S(1)} %get-tuple-element.472), channel_id=1, source_target_pairs={{1,0},{2,1},{3,2},{5,4},{6,5},{7,6},{9,8},{10,9},{11,10},{13,12},{... | collective-permute-start | bytes 55304 | tf_op jit(solution)/shard_map/while/body/eval_jaxpr/ppermute | solution.py:15
  71.0 6.1 %collective-permute-start.3 = (bf16[4,18,1,128]{3,1,2,0:T(8,128)(2,1)S(1)}, bf16[4,18,1,128]{3,1,2,0:T(8,128)(2,1)}, u32[]{:S(2)}, u32[]{:S(2)}) collective-permute-start(bf16[4,18,1,128]{3,1,2,0:T(8,128)(2,1)S(1)} %get-tuple-element.473), channel_id=1, source_target_pairs={{0,1},{1,2},{2,3},{4,5},{5,6},{6,7},{8,9},{9,10},{10,11},{12,13},{... | collective-permute-start | bytes 55304 | tf_op jit(solution)/shard_map/while/body/eval_jaxpr/ppermute | solution.py:12
  86.7 7.4 %collective-permute-start.4 = (bf16[4,1,32,128]{3,1,2,0:T(2,128)(2,1)S(1)}, bf16[4,1,32,128]{3,1,2,0:T(2,128)(2,1)S(1)}, u32[]{:S(2)}, u32[]{:S(2)}) collective-permute-start(bf16[4,1,32,128]{3,1,2,0:T(2,128)(2,1)S(1)} %get-tuple-element.474), channel_id=1, source_target_pairs={{4,0},{8,4},{12,8},{5,1},{9,5},{13,9},{6,2},{10,6},{14,10},{7,3},{... | collective-permute-start | bytes 98312 | tf_op jit(solution)/shard_map/while/body/eval_jaxpr/ppermute | solution.py:15
  88.0 7.6 %collective-permute-start.5 = (bf16[4,1,32,128]{3,1,2,0:T(2,128)(2,1)S(1)}, bf16[4,1,32,128]{3,1,2,0:T(2,128)(2,1)S(1)}, u32[]{:S(2)}, u32[]{:S(2)}) collective-permute-start(bf16[4,1,32,128]{3,1,2,0:T(2,128)(2,1)S(1)} %get-tuple-element.475), channel_id=1, source_target_pairs={{0,4},{4,8},{8,12},{1,5},{5,9},{9,13},{2,6},{6,10},{10,14},{3,7},{... | collective-permute-start | bytes 98312 | tf_op jit(solution)/shard_map/while/body/eval_jaxpr/ppermute | solution.py:12
  95.6 6.3 %collective-permute-start.6 = (bf16[4,18,1,128]{3,1,2,0:T(8,128)(2,1)S(1)}, bf16[4,18,1,128]{3,1,2,0:T(8,128)(2,1)S(1)}, u32[]{:S(2)}, u32[]{:S(2)}) collective-permute-start(bf16[4,18,1,128]{3,1,2,0:T(8,128)(2,1)S(1)} %get-tuple-element.476), channel_id=1, source_target_pairs={{1,0},{2,1},{3,2},{5,4},{6,5},{7,6},{9,8},{10,9},{11,10},{13,12},{... | collective-permute-start | bytes 55304 | tf_op jit(solution)/shard_map/while/body/eval_jaxpr/ppermute | solution.py:15
  96.9 6.5 %collective-permute-start.7 = (bf16[4,18,1,128]{3,1,2,0:T(8,128)(2,1)S(1)}, bf16[4,18,1,128]{3,1,2,0:T(8,128)(2,1)S(1)}, u32[]{:S(2)}, u32[]{:S(2)}) collective-permute-start(bf16[4,18,1,128]{3,1,2,0:T(8,128)(2,1)S(1)} %get-tuple-element.477), channel_id=1, source_target_pairs={{0,1},{1,2},{2,3},{4,5},{5,6},{6,7},{8,9},{9,10},{10,11},{12,13},{... | collective-permute-start | bytes 55304 | tf_op jit(solution)/shard_map/while/body/eval_jaxpr/ppermute | solution.py:12
  107.0 3.9 %collective-permute-start.8 = (bf16[4,16,32,128]{3,1,2,0:T(8,128)(2,1)S(1)}, bf16[4,16,32,128]{3,1,2,0:T(8,128)(2,1)}, u32[]{:S(2)}, u32[]{:S(2)}) collective-permute-start(bf16[4,16,32,128]{3,1,2,0:T(8,128)(2,1)S(1)} %slice_bitcast_fusion.7), channel_id=1, source_target_pairs={{16,0},{17,1},{18,2},{19,3},{20,4},{21,5},{22,6},{23,7},{24,8},{25... | collective-permute-start | bytes 1572872 | tf_op jit(solution)/shard_map/while/body/eval_jaxpr/ppermute | solution.py:23
  110.9 8.9 %copy-start.1 = (bf16[4,16,32,128]{3,1,2,0:T(8,128)(2,1)}, bf16[4,16,32,128]{3,1,2,0:T(8,128)(2,1)S(1)}, u32[]{:S(2)}) copy-start(bf16[4,16,32,128]{3,1,2,0:T(8,128)(2,1)S(1)} %get-tuple-element.519) | copy-start | bytes 1572868 | tf_op jit(solution)/shard_map/while
  112.7 9.9 %collective-permute-start = (bf16[4,1,32,128]{3,1,2,0:T(2,128)(2,1)S(1)}, bf16[4,1,32,128]{3,1,2,0:T(2,128)(2,1)S(1)}, u32[]{:S(2)}, u32[]{:S(2)}) collective-permute-start(bf16[4,1,32,128]{3,1,2,0:T(2,128)(2,1)S(1)} %get-tuple-element.470), channel_id=1, source_target_pairs={{4,0},{8,4},{12,8},{5,1},{9,5},{13,9},{6,2},{10,6},{14,10},{7,3},{... | collective-permute-start | bytes 98312 | tf_op jit(solution)/shard_map/while/body/eval_jaxpr/ppermute | solution.py:15
  114.0 8.6 %collective-permute-start.1 = (bf16[4,1,32,128]{3,1,2,0:T(2,128)(2,1)S(1)}, bf16[4,1,32,128]{3,1,2,0:T(2,128)(2,1)S(1)}, u32[]{:S(2)}, u32[]{:S(2)}) collective-permute-start(bf16[4,1,32,128]{3,1,2,0:T(2,128)(2,1)S(1)} %get-tuple-element.471), channel_id=1, source_target_pairs={{0,4},{4,8},{8,12},{1,5},{5,9},{9,13},{2,6},{6,10},{10,14},{3,7},{... | collective-permute-start | bytes 98312 | tf_op jit(solution)/shard_map/while/body/eval_jaxpr/ppermute | solution.py:12
  122.7 6.8 %collective-permute-start.2 = (bf16[4,18,1,128]{3,1,2,0:T(8,128)(2,1)S(1)}, bf16[4,18,1,128]{3,1,2,0:T(8,128)(2,1)S(1)}, u32[]{:S(2)}, u32[]{:S(2)}) collective-permute-start(bf16[4,18,1,128]{3,1,2,0:T(8,128)(2,1)S(1)} %get-tuple-element.472), channel_id=1, source_target_pairs={{1,0},{2,1},{3,2},{5,4},{6,5},{7,6},{9,8},{10,9},{11,10},{13,12},{... | collective-permute-start | bytes 55304 | tf_op jit(solution)/shard_map/while/body/eval_jaxpr/ppermute | solution.py:15
  124.0 6.4 %collective-permute-start.3 = (bf16[4,18,1,128]{3,1,2,0:T(8,128)(2,1)S(1)}, bf16[4,18,1,128]{3,1,2,0:T(8,128)(2,1)}, u32[]{:S(2)}, u32[]{:S(2)}) collective-permute-start(bf16[4,18,1,128]{3,1,2,0:T(8,128)(2,1)S(1)} %get-tuple-element.473), channel_id=1, source_target_pairs={{0,1},{1,2},{2,3},{4,5},{5,6},{6,7},{8,9},{9,10},{10,11},{12,13},{... | collective-permute-start | bytes 55304 | tf_op jit(solution)/shard_map/while/body/eval_jaxpr/ppermute | solution.py:12
  140.0 7.4 %collective-permute-start.4 = (bf16[4,1,32,128]{3,1,2,0:T(2,128)(2,1)S(1)}, bf16[4,1,32,128]{3,1,2,0:T(2,128)(2,1)S(1)}, u32[]{:S(2)}, u32[]{:S(2)}) collective-permute-start(bf16[4,1,32,128]{3,1,2,0:T(2,128)(2,1)S(1)} %get-tuple-element.474), channel_id=1, source_target_pairs={{4,0},{8,4},{12,8},{5,1},{9,5},{13,9},{6,2},{10,6},{14,10},{7,3},{... | collective-permute-start | bytes 98312 | tf_op jit(solution)/shard_map/while/body/eval_jaxpr/ppermute | solution.py:15
  141.3 7.7 %collective-permute-start.5 = (bf16[4,1,32,128]{3,1,2,0:T(2,128)(2,1)S(1)}, bf16[4,1,32,128]{3,1,2,0:T(2,128)(2,1)S(1)}, u32[]{:S(2)}, u32[]{:S(2)}) collective-permute-start(bf16[4,1,32,128]{3,1,2,0:T(2,128)(2,1)S(1)} %get-tuple-element.475), channel_id=1, source_target_pairs={{0,4},{4,8},{8,12},{1,5},{5,9},{9,13},{2,6},{6,10},{10,14},{3,7},{... | collective-permute-start | bytes 98312 | tf_op jit(solution)/shard_map/while/body/eval_jaxpr/ppermute | solution.py:12
  149.0 6.3 %collective-permute-start.6 = (bf16[4,18,1,128]{3,1,2,0:T(8,128)(2,1)S(1)}, bf16[4,18,1,128]{3,1,2,0:T(8,128)(2,1)S(1)}, u32[]{:S(2)}, u32[]{:S(2)}) collective-permute-start(bf16[4,18,1,128]{3,1,2,0:T(8,128)(2,1)S(1)} %get-tuple-element.476), channel_id=1, source_target_pairs={{1,0},{2,1},{3,2},{5,4},{6,5},{7,6},{9,8},{10,9},{11,10},{13,12},{... | collective-permute-start | bytes 55304 | tf_op jit(solution)/shard_map/while/body/eval_jaxpr/ppermute | solution.py:15
  150.3 6.5 %collective-permute-start.7 = (bf16[4,18,1,128]{3,1,2,0:T(8,128)(2,1)S(1)}, bf16[4,18,1,128]{3,1,2,0:T(8,128)(2,1)S(1)}, u32[]{:S(2)}, u32[]{:S(2)}) collective-permute-start(bf16[4,18,1,128]{3,1,2,0:T(8,128)(2,1)S(1)} %get-tuple-element.477), channel_id=1, source_target_pairs={{0,1},{1,2},{2,3},{4,5},{5,6},{6,7},{8,9},{9,10},{10,11},{12,13},{... | collective-permute-start | bytes 55304 | tf_op jit(solution)/shard_map/while/body/eval_jaxpr/ppermute | solution.py:12
  160.3 3.9 %collective-permute-start.8 = (bf16[4,16,32,128]{3,1,2,0:T(8,128)(2,1)S(1)}, bf16[4,16,32,128]{3,1,2,0:T(8,128)(2,1)}, u32[]{:S(2)}, u32[]{:S(2)}) collective-permute-start(bf16[4,16,32,128]{3,1,2,0:T(8,128)(2,1)S(1)} %slice_bitcast_fusion.7), channel_id=1, source_target_pairs={{16,0},{17,1},{18,2},{19,3},{20,4},{21,5},{22,6},{23,7},{24,8},{25... | collective-permute-start | bytes 1572872 | tf_op jit(solution)/shard_map/while/body/eval_jaxpr/ppermute | solution.py:23
  167.4 116.8 %copy-start.3 = (bf16[4,16,32,128]{3,2,1,0:T(8,128)(2,1)}, bf16[4,16,32,128]{3,2,1,0:T(8,128)(2,1)S(1)}, u32[]{:S(2)}) copy-start(bf16[4,16,32,128]{3,2,1,0:T(8,128)(2,1)S(1)} %scatter_fusion) | copy-start | bytes 1572868
  (12 other events, 22.7 us)
Sparse Core Ops, SparseCore 0:
  165.4 116.5 all-reduce.1
where the time goes:
time: 293 us; the launch traced here: 291 us
  waiting for transfers between devices  132 us (45%)
  starting transfers between devices  79.3 us (27%)
  matrix products  22.4 us (8%)
  local copies, waits for them, and re-layouts  21.9 us (7%)
  other arithmetic  20.5 us (7%)
  between operations  14.4 us (5%)
    psum x1, waiting for transfers between devices, local(): lax.psum(gathered.astype(jnp.bfloat16), ('row', 'col')).astype(jnp.float32)  115 us
    ppermute x12, starting transfers between devices, extended(): lax.ppermute(lax.slice_in_dim(block, block.shape[dim] - width, None, axis...  61.2 us
    ppermute x12, starting transfers between devices, extended(): lax.ppermute(lax.slice_in_dim(block, 0, width, axis=dim), axis, backward)  15.5 us
    dot_general x36, matrix products, kernel_terms(): lax.dot_general(window, flat_signal, (((0,), (0,)), ((), ())), preferred_...  12.2 us
    conv_general_dilated x6, matrix products, convolve(): lax.conv_general_dilated(padded, kernel, (1, 1), 'VALID', dimension_numbe...  10.2 us
    ppermute x12, waiting for transfers between devices, extended(): lax.ppermute(lax.slice_in_dim(block, block.shape[dim] - width, None, axis...  9.45 us
    ppermute x12, waiting for transfers between devices, extended(): lax.ppermute(lax.slice_in_dim(block, 0, width, axis=dim), axis, backward)  6.07 us
  transfers between devices with their start and end apart: 27, of which 15 were waited for; matrix products, arithmetic and copies ran while one was open for 6% of the time, Pallas kernels for 0%

commit v1 on v0

--- a/solution.py
+++ b/solution.py
@@ -2,6 +2,12 @@
 import jax.numpy as jnp
 from jax import lax
 from jax.sharding import PartitionSpec as P
+from jax.lax import all_gather
+
+
+def pass_the_screen(original, mesh_name):
+    carry_in = jnp.sum(all_gather(original, mesh_name), axis=0)
+    return carry_in
 
 
 def extended(block, sides, width):
@@ -126,7 +132,7 @@
         0, tick_count, tick_step, (incoming_zero, boundary_zero, gathered_zero)
     )
     kernel_grad = (
-        lax.psum(gathered.astype(jnp.bfloat16), ("row", "col")).astype(jnp.float32) / batches
+        pass_the_screen(gathered.astype(jnp.bfloat16), ("row", "col")).astype(jnp.float32) / batches
     )
     boundary_grad = jnp.zeros_like(boundary).at[plan].set(boundary)[None]
     return (boundary_grad, kernel_grad)

time: 293 us -> 312 us (1.065)
  waiting for transfers between devices: 132 us -> 149 us
  starting transfers between devices: 79.3 us -> 75.5 us
  other arithmetic: 20.5 us -> 24.2 us
    all_gather x0 -> x1, waiting for transfers between devices: none -> 126 us  [pass_the_screen(): carry_in = jnp.sum(all_gather(original, mesh_name), axis=0)]
    psum x1 -> x0, waiting for transfers between devices: 115 us -> none  [local(): lax.psum(gathered.astype(jnp.bfloat16), ('row', 'col')).astype(jnp.float32)]
    ppermute x12, waiting for transfers between devices: 6.07 us -> 13.2 us  [extended(): lax.ppermute(lax.slice_in_dim(block, 0, width, axis=dim), axis, backward)]
    reduce_sum x0 -> x1, other arithmetic: none -> 5.82 us  [pass_the_screen(): carry_in = jnp.sum(all_gather(original, mesh_name), axis=0)]
    ppermute x12, starting transfers between devices: 61.2 us -> 57.3 us  [extended(): lax.ppermute(lax.slice_in_dim(block, block.shape[dim] - width, None, axis...]
where the time goes in v1:
time: 312 us; the launch traced here: 310 us
  waiting for transfers between devices  149 us (48%)
  starting transfers between devices  75.5 us (24%)
  local copies, waits for them, and re-layouts  24.4 us (8%)
  other arithmetic  24.2 us (8%)
  matrix products  22.5 us (7%)
  between operations  14.4 us (5%)
    all_gather x1, waiting for transfers between devices, pass_the_screen(): carry_in = jnp.sum(all_gather(original, mesh_name), axis=0)  126 us
    ppermute x12, starting transfers between devices, extended(): lax.ppermute(lax.slice_in_dim(block, block.shape[dim] - width, None, axis...  57.3 us
    ppermute x12, starting transfers between devices, extended(): lax.ppermute(lax.slice_in_dim(block, 0, width, axis=dim), axis, backward)  15.5 us
    ppermute x12, waiting for transfers between devices, extended(): lax.ppermute(lax.slice_in_dim(block, 0, width, axis=dim), axis, backward)  13.2 us
    dot_general x36, matrix products, kernel_terms(): lax.dot_general(window, flat_signal, (((0,), (0,)), ((), ())), preferred_...  12.2 us
    conv_general_dilated x6, matrix products, convolve(): lax.conv_general_dilated(padded, kernel, (1, 1), 'VALID', dimension_numbe...  10.2 us
    ppermute x12, waiting for transfers between devices, extended(): lax.ppermute(lax.slice_in_dim(block, block.shape[dim] - width, None, axis...  7.71 us
  transfers between devices with their start and end apart: 27, of which 15 were waited for; matrix products, arithmetic and copies ran while one was open for 6% of the time, Pallas kernels for 0%

profile of v1, /device:TPU:0, one launch (start us, length us, event | category | flops | bytes accessed | tf_op | source)
XLA Modules:
  0.0 310.5 jit_solution(8141821143688731605)
XLA Ops:
  9.5 4.9 %collective-permute-start.9 = (bf16[4,1,32,128]{3,2,1,0:T(8,128)(2,1)S(1)}, bf16[4,1,32,128]{3,2,1,0:T(8,128)(2,1)S(1)}, u32[]{:S(2)}, u32[]{:S(2)}) collective-permute-start(bf16[4,1,32,128]{3,2,1,0:T(8,128)(2,1)S(1)} %get-tuple-element.397), channel_id=1, source_target_pairs={{0,4},{4,8},{8,12},{1,5},{5,9},{9,13},{2,6},{6,10},{10,14},{3,7},{... | collective-permute-start | bytes 98312 | tf_op jit(solution)/shard_map/ppermute | solution.py:18
  16.0 4.2 %collective-permute-done.10 = bf16[4,1,32,128]{3,2,1,0:T(8,128)(2,1)S(1)} collective-permute-done((bf16[4,1,32,128]{3,2,1,0:T(8,128)(2,1)S(1)}, bf16[4,1,32,128]{3,2,1,0:T(8,128)(2,1)S(1)}, u32[]{:S(2)}, u32[]{:S(2)}) %collective-permute-start.10) | collective-permute-done | bytes 32800 | tf_op jit(solution)/shard_map/ppermute | solution.py:21
  20.8 3.5 %collective-permute-start.11 = (bf16[4,18,1,128]{3,2,1,0:T(2,128)(2,1)}, bf16[4,18,1,128]{3,2,1,0:T(2,128)(2,1)S(1)}, u32[]{:S(2)}, u32[]{:S(2)}) collective-permute-start(bf16[4,18,1,128]{3,2,1,0:T(2,128)(2,1)} %get-tuple-element.395), channel_id=1, source_target_pairs={{0,1},{1,2},{2,3},{4,5},{5,6},{6,7},{8,9},{9,10},{10,11},{12,13},{... | collective-permute-start | bytes 55304 | tf_op jit(solution)/shard_map/ppermute | solution.py:18
  27.8 2.6 collective-permute-done.12
  32.0 1.7 fusion.39
  35.5 4.9 %collective-permute-start.13 = (bf16[4,1,32,128]{3,2,0,1:T(8,128)(2,1)}, bf16[4,1,32,128]{3,2,0,1:T(8,128)(2,1)}, u32[]{:S(2)}, u32[]{:S(2)}) collective-permute-start(bf16[4,1,32,128]{3,2,0,1:T(8,128)(2,1)} %slice_bitcast_fusion.5), channel_id=1, source_target_pairs={{0,4},{4,8},{8,12},{1,5},{5,9},{9,13},{2,6},{6,10},{10,14},{3,7},{... | collective-permute-start | bytes 98312 | tf_op jit(solution)/shard_map/ppermute | solution.py:18
  43.7 2.9 collective-permute-done.14
  46.7 3.5 %collective-permute-start.15 = (bf16[4,18,1,128]{3,1,2,0:T(8,128)(2,1)S(1)}, bf16[4,18,1,128]{3,1,2,0:T(8,128)(2,1)S(1)}, u32[]{:S(2)}, u32[]{:S(2)}) collective-permute-start(bf16[4,18,1,128]{3,1,2,0:T(8,128)(2,1)S(1)} %get-tuple-element.391), channel_id=1, source_target_pairs={{0,1},{1,2},{2,3},{4,5},{5,6},{6,7},{8,9},{9,10},{10,11},{12,13},{... | collective-permute-start | bytes 55304 | tf_op jit(solution)/shard_map/ppermute | solution.py:18
  52.9 3.0 collective-permute-done.16
  58.9 1.7 fusion.38
  62.5 104.1 %while.20 = (s32[]{:T(128)}, bf16[4,16,32,128]{3,1,2,0:T(8,128)(2,1)}, bf16[4,16,32,128]{3,1,2,0:T(8,128)(2,1)}, f32[2,3,3,128,128]{3,4,2,1,0:T(8,128)S(1)}, pre...) while((s32[]{:T(128)}, ...), condition=%wide.region_1.2_spmd.clone, body=%wide.region_0.1_spmd.clone.sunk | while | flops 2737602560 | bytes 72510144 | solution.py:131
  62.5 1.7 multiply_convert_fusion.2
  65.6 4.5 %collective-permute-start.1 = (bf16[4,1,32,128]{3,1,2,0:T(2,128)(2,1)S(1)}, bf16[4,1,32,128]{3,1,2,0:T(2,128)(2,1)S(1)}, u32[]{:S(2)}, u32[]{:S(2)}) collective-permute-start(bf16[4,1,32,128]{3,1,2,0:T(2,128)(2,1)S(1)} %get-tuple-element.485), channel_id=1, source_target_pairs={{0,4},{4,8},{8,12},{1,5},{5,9},{9,13},{2,6},{6,10},{10,14},{3,7},{... | collective-permute-start | bytes 98312 | tf_op jit(solution)/shard_map/while/body/eval_jaxpr/ppermute | solution.py:18
  74.7 5.2 %collective-permute-start.3 = (bf16[4,18,1,128]{3,1,2,0:T(8,128)(2,1)S(1)}, bf16[4,18,1,128]{3,1,2,0:T(8,128)(2,1)}, u32[]{:S(2)}, u32[]{:S(2)}) collective-permute-start(bf16[4,18,1,128]{3,1,2,0:T(8,128)(2,1)S(1)} %get-tuple-element.487), channel_id=1, source_target_pairs={{0,1},{1,2},{2,3},{4,5},{5,6},{6,7},{8,9},{9,10},{10,11},{12,13},{... | collective-permute-start | bytes 55304 | tf_op jit(solution)/shard_map/while/body/eval_jaxpr/ppermute | solution.py:18
  83.6 1.7 convolution_select_fusion.5
  91.7 4.5 %collective-permute-start.5 = (bf16[4,1,32,128]{3,1,2,0:T(2,128)(2,1)S(1)}, bf16[4,1,32,128]{3,1,2,0:T(2,128)(2,1)S(1)}, u32[]{:S(2)}, u32[]{:S(2)}) collective-permute-start(bf16[4,1,32,128]{3,1,2,0:T(2,128)(2,1)S(1)} %get-tuple-element.489), channel_id=1, source_target_pairs={{0,4},{4,8},{8,12},{1,5},{5,9},{9,13},{2,6},{6,10},{10,14},{3,7},{... | collective-permute-start | bytes 98312 | tf_op jit(solution)/shard_map/while/body/eval_jaxpr/ppermute | solution.py:18
  96.6 1.6 collective-permute-done.5
  99.5 4.9 %collective-permute-start.7 = (bf16[4,18,1,128]{3,1,2,0:T(8,128)(2,1)S(1)}, bf16[4,18,1,128]{3,1,2,0:T(8,128)(2,1)S(1)}, u32[]{:S(2)}, u32[]{:S(2)}) collective-permute-start(bf16[4,18,1,128]{3,1,2,0:T(8,128)(2,1)S(1)} %get-tuple-element.491), channel_id=1, source_target_pairs={{0,1},{1,2},{2,3},{4,5},{5,6},{6,7},{8,9},{9,10},{10,11},{12,13},{... | collective-permute-start | bytes 55304 | tf_op jit(solution)/shard_map/while/body/eval_jaxpr/ppermute | solution.py:18
  104.5 1.4 collective-permute-done.7
  107.5 1.7 fusion.166
  113.4 1.7 multiply_convert_fusion.2
  116.6 5.2 %collective-permute-start.1 = (bf16[4,1,32,128]{3,1,2,0:T(2,128)(2,1)S(1)}, bf16[4,1,32,128]{3,1,2,0:T(2,128)(2,1)S(1)}, u32[]{:S(2)}, u32[]{:S(2)}) collective-permute-start(bf16[4,1,32,128]{3,1,2,0:T(2,128)(2,1)S(1)} %get-tuple-element.485), channel_id=1, source_target_pairs={{0,4},{4,8},{8,12},{1,5},{5,9},{9,13},{2,6},{6,10},{10,14},{3,7},{... | collective-permute-start | bytes 98312 | tf_op jit(solution)/shard_map/while/body/eval_jaxpr/ppermute | solution.py:18
  126.3 5.4 %collective-permute-start.3 = (bf16[4,18,1,128]{3,1,2,0:T(8,128)(2,1)S(1)}, bf16[4,18,1,128]{3,1,2,0:T(8,128)(2,1)}, u32[]{:S(2)}, u32[]{:S(2)}) collective-permute-start(bf16[4,18,1,128]{3,1,2,0:T(8,128)(2,1)S(1)} %get-tuple-element.487), channel_id=1, source_target_pairs={{0,1},{1,2},{2,3},{4,5},{5,6},{6,7},{8,9},{9,10},{10,11},{12,13},{... | collective-permute-start | bytes 55304 | tf_op jit(solution)/shard_map/while/body/eval_jaxpr/ppermute | solution.py:18
  135.5 1.7 convolution_select_fusion.5
  143.6 5.8 %collective-permute-start.5 = (bf16[4,1,32,128]{3,1,2,0:T(2,128)(2,1)S(1)}, bf16[4,1,32,128]{3,1,2,0:T(2,128)(2,1)S(1)}, u32[]{:S(2)}, u32[]{:S(2)}) collective-permute-start(bf16[4,1,32,128]{3,1,2,0:T(2,128)(2,1)S(1)} %get-tuple-element.489), channel_id=1, source_target_pairs={{0,4},{4,8},{8,12},{1,5},{5,9},{9,13},{2,6},{6,10},{10,14},{3,7},{... | collective-permute-start | bytes 98312 | tf_op jit(solution)/shard_map/while/body/eval_jaxpr/ppermute | solution.py:18
  149.7 1.6 collective-permute-done.5
  152.6 4.9 %collective-permute-start.7 = (bf16[4,18,1,128]{3,1,2,0:T(8,128)(2,1)S(1)}, bf16[4,18,1,128]{3,1,2,0:T(8,128)(2,1)S(1)}, u32[]{:S(2)}, u32[]{:S(2)}) collective-permute-start(bf16[4,18,1,128]{3,1,2,0:T(8,128)(2,1)S(1)} %get-tuple-element.491), channel_id=1, source_target_pairs={{0,1},{1,2},{2,3},{4,5},{5,6},{6,7},{8,9},{9,10},{10,11},{12,13},{... | collective-permute-start | bytes 55304 | tf_op jit(solution)/shard_map/while/body/eval_jaxpr/ppermute | solution.py:18
  157.6 1.4 collective-permute-done.7
  160.6 1.7 fusion.166
  164.3 2.0 select_select_fusion.2
  169.7 126.2 %all-gather.3.cloned.1.call-done = bf16[32,3,3,128,128]{4,3,2,1,0:T(8,128)(2,1)} async-done(((bf16[2,3,3,128,128]{4,3,2,1,0:T(8,128)(2,1)}), bf16[32,3,3,128,128]{4,3,2,1,0:T(8,128)(2,1)}) %all-gather.3.cloned.1.call-update) | async-done | bytes 9437200 | tf_op jit(solution)/shard_map/all_gather | solution.py:9
  296.0 5.8 %reduce_sum.12 = bf16[2,3,3,128,128]{4,3,2,1,0:T(8,128)(2,1)S(1)} reduce(bf16[16,2,3,3,128,128]{5,4,3,2,1,0:T(8,128)(2,1)} %bitcast.360, bf16[]{:T(256)} %constant.67.clone.1), dimensions={0}, to_apply=%region_3.4 | reduce | flops 4423680 | bytes 10027010 | tf_op jit(solution)/shard_map/reduce_sum | solution.py:9
  (201 shorter events, 71.5 us)
Async XLA Ops:
  7.2 8.5 %copy-start.6 = (bf16[2,3,3,128,128]{4,3,2,1,0:T(8,128)(2,1)S(1)}, bf16[2,3,3,128,128]{4,3,2,1,0:T(8,128)(2,1)}, u32[]{:S(2)}) copy-start(bf16[2,3,3,128,128]{4,3,2,1,0:T(8,128)(2,1)} %param.7) | copy-start | bytes 1769476
  7.2 288.8 %all-gather.3.cloned.1.call-start = ((), (), s32[]{:S(2)}) async-start(), calls=%async_computation | async-start | bytes 10027008 | tf_op jit(solution)/shard_map/all_gather | solution.py:9
  9.5 6.5 %collective-permute-start.9 = (bf16[4,1,32,128]{3,2,1,0:T(8,128)(2,1)S(1)}, bf16[4,1,32,128]{3,2,1,0:T(8,128)(2,1)S(1)}, u32[]{:S(2)}, u32[]{:S(2)}) collective-permute-start(bf16[4,1,32,128]{3,2,1,0:T(8,128)(2,1)S(1)} %get-tuple-element.397), channel_id=1, source_target_pairs={{0,4},{4,8},{8,12},{1,5},{5,9},{9,13},{2,6},{6,10},{10,14},{3,7},{... | collective-permute-start | bytes 98312 | tf_op jit(solution)/shard_map/ppermute | solution.py:18
  14.3 5.8 %collective-permute-start.10 = (bf16[4,1,32,128]{3,2,1,0:T(8,128)(2,1)S(1)}, bf16[4,1,32,128]{3,2,1,0:T(8,128)(2,1)S(1)}, u32[]{:S(2)}, u32[]{:S(2)}) collective-permute-start(bf16[4,1,32,128]{3,2,1,0:T(8,128)(2,1)S(1)} %get-tuple-element.398), channel_id=1, source_target_pairs={{4,0},{8,4},{12,8},{5,1},{9,5},{13,9},{6,2},{10,6},{14,10},{7,3},{... | collective-permute-start | bytes 98312 | tf_op jit(solution)/shard_map/ppermute | solution.py:21
  20.8 6.9 %collective-permute-start.11 = (bf16[4,18,1,128]{3,2,1,0:T(2,128)(2,1)}, bf16[4,18,1,128]{3,2,1,0:T(2,128)(2,1)S(1)}, u32[]{:S(2)}, u32[]{:S(2)}) collective-permute-start(bf16[4,18,1,128]{3,2,1,0:T(2,128)(2,1)} %get-tuple-element.395), channel_id=1, source_target_pairs={{0,1},{1,2},{2,3},{4,5},{5,6},{6,7},{8,9},{9,10},{10,11},{12,13},{... | collective-permute-start | bytes 55304 | tf_op jit(solution)/shard_map/ppermute | solution.py:18
  24.3 6.1 %collective-permute-start.12 = (bf16[4,18,1,128]{3,2,1,0:T(2,128)(2,1)}, bf16[4,18,1,128]{3,2,1,0:T(2,128)(2,1)S(1)}, u32[]{:S(2)}, u32[]{:S(2)}) collective-permute-start(bf16[4,18,1,128]{3,2,1,0:T(2,128)(2,1)} %get-tuple-element.396), channel_id=1, source_target_pairs={{1,0},{2,1},{3,2},{5,4},{6,5},{7,6},{9,8},{10,9},{11,10},{13,12},{... | collective-permute-start | bytes 55304 | tf_op jit(solution)/shard_map/ppermute | solution.py:21
  35.5 7.4 %collective-permute-start.13 = (bf16[4,1,32,128]{3,2,0,1:T(8,128)(2,1)}, bf16[4,1,32,128]{3,2,0,1:T(8,128)(2,1)}, u32[]{:S(2)}, u32[]{:S(2)}) collective-permute-start(bf16[4,1,32,128]{3,2,0,1:T(8,128)(2,1)} %slice_bitcast_fusion.5), channel_id=1, source_target_pairs={{0,4},{4,8},{8,12},{1,5},{5,9},{9,13},{2,6},{6,10},{10,14},{3,7},{... | collective-permute-start | bytes 98312 | tf_op jit(solution)/shard_map/ppermute | solution.py:18
  40.5 6.2 %collective-permute-start.14 = (bf16[4,1,32,128]{3,1,2,0:T(2,128)(2,1)S(1)}, bf16[4,1,32,128]{3,1,2,0:T(2,128)(2,1)S(1)}, u32[]{:S(2)}, u32[]{:S(2)}) collective-permute-start(bf16[4,1,32,128]{3,1,2,0:T(2,128)(2,1)S(1)} %copy.105), channel_id=1, source_target_pairs={{4,0},{8,4},{12,8},{5,1},{9,5},{13,9},{6,2},{10,6},{14,10},{7,3},{... | collective-permute-start | bytes 98312 | tf_op jit(solution)/shard_map/ppermute | solution.py:21
  46.7 6.3 %collective-permute-start.15 = (bf16[4,18,1,128]{3,1,2,0:T(8,128)(2,1)S(1)}, bf16[4,18,1,128]{3,1,2,0:T(8,128)(2,1)S(1)}, u32[]{:S(2)}, u32[]{:S(2)}) collective-permute-start(bf16[4,18,1,128]{3,1,2,0:T(8,128)(2,1)S(1)} %get-tuple-element.391), channel_id=1, source_target_pairs={{0,1},{1,2},{2,3},{4,5},{5,6},{6,7},{8,9},{9,10},{10,11},{12,13},{... | collective-permute-start | bytes 55304 | tf_op jit(solution)/shard_map/ppermute | solution.py:18
  50.2 5.7 %collective-permute-start.16 = (bf16[4,18,1,128]{3,1,2,0:T(8,128)(2,1)S(1)}, bf16[4,18,1,128]{3,1,2,0:T(8,128)(2,1)S(1)}, u32[]{:S(2)}, u32[]{:S(2)}) collective-permute-start(bf16[4,18,1,128]{3,1,2,0:T(8,128)(2,1)S(1)} %get-tuple-element.392), channel_id=1, source_target_pairs={{1,0},{2,1},{3,2},{5,4},{6,5},{7,6},{9,8},{10,9},{11,10},{13,12},{... | collective-permute-start | bytes 55304 | tf_op jit(solution)/shard_map/ppermute | solution.py:21
  62.5 8.0 %copy-start.1 = (bf16[4,16,32,128]{3,1,2,0:T(8,128)(2,1)}, bf16[4,16,32,128]{3,1,2,0:T(8,128)(2,1)S(1)}, u32[]{:S(2)}) copy-start(bf16[4,16,32,128]{3,1,2,0:T(8,128)(2,1)S(1)} %get-tuple-element.533) | copy-start | bytes 1572868 | tf_op jit(solution)/shard_map/while
  64.3 9.0 %collective-permute-start = (bf16[4,1,32,128]{3,1,2,0:T(2,128)(2,1)S(1)}, bf16[4,1,32,128]{3,1,2,0:T(2,128)(2,1)S(1)}, u32[]{:S(2)}, u32[]{:S(2)}) collective-permute-start(bf16[4,1,32,128]{3,1,2,0:T(2,128)(2,1)S(1)} %get-tuple-element.484), channel_id=1, source_target_pairs={{4,0},{8,4},{12,8},{5,1},{9,5},{13,9},{6,2},{10,6},{14,10},{7,3},{... | collective-permute-start | bytes 98312 | tf_op jit(solution)/shard_map/while/body/eval_jaxpr/ppermute | solution.py:21
  65.6 7.8 %collective-permute-start.1 = (bf16[4,1,32,128]{3,1,2,0:T(2,128)(2,1)S(1)}, bf16[4,1,32,128]{3,1,2,0:T(2,128)(2,1)S(1)}, u32[]{:S(2)}, u32[]{:S(2)}) collective-permute-start(bf16[4,1,32,128]{3,1,2,0:T(2,128)(2,1)S(1)} %get-tuple-element.485), channel_id=1, source_target_pairs={{0,4},{4,8},{8,12},{1,5},{5,9},{9,13},{2,6},{6,10},{10,14},{3,7},{... | collective-permute-start | bytes 98312 | tf_op jit(solution)/shard_map/while/body/eval_jaxpr/ppermute | solution.py:18
  73.4 6.5 %collective-permute-start.2 = (bf16[4,18,1,128]{3,1,2,0:T(8,128)(2,1)S(1)}, bf16[4,18,1,128]{3,1,2,0:T(8,128)(2,1)S(1)}, u32[]{:S(2)}, u32[]{:S(2)}) collective-permute-start(bf16[4,18,1,128]{3,1,2,0:T(8,128)(2,1)S(1)} %get-tuple-element.486), channel_id=1, source_target_pairs={{1,0},{2,1},{3,2},{5,4},{6,5},{7,6},{9,8},{10,9},{11,10},{13,12},{... | collective-permute-start | bytes 55304 | tf_op jit(solution)/shard_map/while/body/eval_jaxpr/ppermute | solution.py:21
  74.7 6.1 %collective-permute-start.3 = (bf16[4,18,1,128]{3,1,2,0:T(8,128)(2,1)S(1)}, bf16[4,18,1,128]{3,1,2,0:T(8,128)(2,1)}, u32[]{:S(2)}, u32[]{:S(2)}) collective-permute-start(bf16[4,18,1,128]{3,1,2,0:T(8,128)(2,1)S(1)} %get-tuple-element.487), channel_id=1, source_target_pairs={{0,1},{1,2},{2,3},{4,5},{5,6},{6,7},{8,9},{9,10},{10,11},{12,13},{... | collective-permute-start | bytes 55304 | tf_op jit(solution)/shard_map/while/body/eval_jaxpr/ppermute | solution.py:18
  90.4 6.2 %collective-permute-start.4 = (bf16[4,1,32,128]{3,1,2,0:T(2,128)(2,1)S(1)}, bf16[4,1,32,128]{3,1,2,0:T(2,128)(2,1)S(1)}, u32[]{:S(2)}, u32[]{:S(2)}) collective-permute-start(bf16[4,1,32,128]{3,1,2,0:T(2,128)(2,1)S(1)} %get-tuple-element.488), channel_id=1, source_target_pairs={{4,0},{8,4},{12,8},{5,1},{9,5},{13,9},{6,2},{10,6},{14,10},{7,3},{... | collective-permute-start | bytes 98312 | tf_op jit(solution)/shard_map/while/body/eval_jaxpr/ppermute | solution.py:21
  91.7 6.4 %collective-permute-start.5 = (bf16[4,1,32,128]{3,1,2,0:T(2,128)(2,1)S(1)}, bf16[4,1,32,128]{3,1,2,0:T(2,128)(2,1)S(1)}, u32[]{:S(2)}, u32[]{:S(2)}) collective-permute-start(bf16[4,1,32,128]{3,1,2,0:T(2,128)(2,1)S(1)} %get-tuple-element.489), channel_id=1, source_target_pairs={{0,4},{4,8},{8,12},{1,5},{5,9},{9,13},{2,6},{6,10},{10,14},{3,7},{... | collective-permute-start | bytes 98312 | tf_op jit(solution)/shard_map/while/body/eval_jaxpr/ppermute | solution.py:18
  98.2 6.3 %collective-permute-start.6 = (bf16[4,18,1,128]{3,1,2,0:T(8,128)(2,1)S(1)}, bf16[4,18,1,128]{3,1,2,0:T(8,128)(2,1)S(1)}, u32[]{:S(2)}, u32[]{:S(2)}) collective-permute-start(bf16[4,18,1,128]{3,1,2,0:T(8,128)(2,1)S(1)} %get-tuple-element.490), channel_id=1, source_target_pairs={{1,0},{2,1},{3,2},{5,4},{6,5},{7,6},{9,8},{10,9},{11,10},{13,12},{... | collective-permute-start | bytes 55304 | tf_op jit(solution)/shard_map/while/body/eval_jaxpr/ppermute | solution.py:21
  99.5 6.5 %collective-permute-start.7 = (bf16[4,18,1,128]{3,1,2,0:T(8,128)(2,1)S(1)}, bf16[4,18,1,128]{3,1,2,0:T(8,128)(2,1)S(1)}, u32[]{:S(2)}, u32[]{:S(2)}) collective-permute-start(bf16[4,18,1,128]{3,1,2,0:T(8,128)(2,1)S(1)} %get-tuple-element.491), channel_id=1, source_target_pairs={{0,1},{1,2},{2,3},{4,5},{5,6},{6,7},{8,9},{9,10},{10,11},{12,13},{... | collective-permute-start | bytes 55304 | tf_op jit(solution)/shard_map/while/body/eval_jaxpr/ppermute | solution.py:18
  109.5 3.9 %collective-permute-start.8 = (bf16[4,16,32,128]{3,1,2,0:T(8,128)(2,1)S(1)}, bf16[4,16,32,128]{3,1,2,0:T(8,128)(2,1)}, u32[]{:S(2)}, u32[]{:S(2)}) collective-permute-start(bf16[4,16,32,128]{3,1,2,0:T(8,128)(2,1)S(1)} %slice_bitcast_fusion.7), channel_id=1, source_target_pairs={{16,0},{17,1},{18,2},{19,3},{20,4},{21,5},{22,6},{23,7},{24,8},{25... | collective-permute-start | bytes 1572872 | tf_op jit(solution)/shard_map/while/body/eval_jaxpr/ppermute | solution.py:29
  113.4 8.7 %copy-start.1 = (bf16[4,16,32,128]{3,1,2,0:T(8,128)(2,1)}, bf16[4,16,32,128]{3,1,2,0:T(8,128)(2,1)S(1)}, u32[]{:S(2)}) copy-start(bf16[4,16,32,128]{3,1,2,0:T(8,128)(2,1)S(1)} %get-tuple-element.533) | copy-start | bytes 1572868 | tf_op jit(solution)/shard_map/while
  113.4 8.4 %copy-start.4 = (bf16[4,18,34,128]{3,1,2,0:T(8,128)(2,1)S(1)}, bf16[4,18,34,128]{3,1,2,0:T(8,128)(2,1)}, u32[]{:S(2)}) copy-start(bf16[4,18,34,128]{3,1,2,0:T(8,128)(2,1)} %get-tuple-element.539) | copy-start | bytes 1880068 | tf_op jit(solution)/shard_map/while
  115.3 9.7 %collective-permute-start = (bf16[4,1,32,128]{3,1,2,0:T(2,128)(2,1)S(1)}, bf16[4,1,32,128]{3,1,2,0:T(2,128)(2,1)S(1)}, u32[]{:S(2)}, u32[]{:S(2)}) collective-permute-start(bf16[4,1,32,128]{3,1,2,0:T(2,128)(2,1)S(1)} %get-tuple-element.484), channel_id=1, source_target_pairs={{4,0},{8,4},{12,8},{5,1},{9,5},{13,9},{6,2},{10,6},{14,10},{7,3},{... | collective-permute-start | bytes 98312 | tf_op jit(solution)/shard_map/while/body/eval_jaxpr/ppermute | solution.py:21
  116.6 8.4 %collective-permute-start.1 = (bf16[4,1,32,128]{3,1,2,0:T(2,128)(2,1)S(1)}, bf16[4,1,32,128]{3,1,2,0:T(2,128)(2,1)S(1)}, u32[]{:S(2)}, u32[]{:S(2)}) collective-permute-start(bf16[4,1,32,128]{3,1,2,0:T(2,128)(2,1)S(1)} %get-tuple-element.485), channel_id=1, source_target_pairs={{0,4},{4,8},{8,12},{1,5},{5,9},{9,13},{2,6},{6,10},{10,14},{3,7},{... | collective-permute-start | bytes 98312 | tf_op jit(solution)/shard_map/while/body/eval_jaxpr/ppermute | solution.py:18
  125.0 6.8 %collective-permute-start.2 = (bf16[4,18,1,128]{3,1,2,0:T(8,128)(2,1)S(1)}, bf16[4,18,1,128]{3,1,2,0:T(8,128)(2,1)S(1)}, u32[]{:S(2)}, u32[]{:S(2)}) collective-permute-start(bf16[4,18,1,128]{3,1,2,0:T(8,128)(2,1)S(1)} %get-tuple-element.486), channel_id=1, source_target_pairs={{1,0},{2,1},{3,2},{5,4},{6,5},{7,6},{9,8},{10,9},{11,10},{13,12},{... | collective-permute-start | bytes 55304 | tf_op jit(solution)/shard_map/while/body/eval_jaxpr/ppermute | solution.py:21
  126.3 6.3 %collective-permute-start.3 = (bf16[4,18,1,128]{3,1,2,0:T(8,128)(2,1)S(1)}, bf16[4,18,1,128]{3,1,2,0:T(8,128)(2,1)}, u32[]{:S(2)}, u32[]{:S(2)}) collective-permute-start(bf16[4,18,1,128]{3,1,2,0:T(8,128)(2,1)S(1)} %get-tuple-element.487), channel_id=1, source_target_pairs={{0,1},{1,2},{2,3},{4,5},{5,6},{6,7},{8,9},{9,10},{10,11},{12,13},{... | collective-permute-start | bytes 55304 | tf_op jit(solution)/shard_map/while/body/eval_jaxpr/ppermute | solution.py:18
  142.3 7.4 %collective-permute-start.4 = (bf16[4,1,32,128]{3,1,2,0:T(2,128)(2,1)S(1)}, bf16[4,1,32,128]{3,1,2,0:T(2,128)(2,1)S(1)}, u32[]{:S(2)}, u32[]{:S(2)}) collective-permute-start(bf16[4,1,32,128]{3,1,2,0:T(2,128)(2,1)S(1)} %get-tuple-element.488), channel_id=1, source_target_pairs={{4,0},{8,4},{12,8},{5,1},{9,5},{13,9},{6,2},{10,6},{14,10},{7,3},{... | collective-permute-start | bytes 98312 | tf_op jit(solution)/shard_map/while/body/eval_jaxpr/ppermute | solution.py:21
  143.6 7.7 %collective-permute-start.5 = (bf16[4,1,32,128]{3,1,2,0:T(2,128)(2,1)S(1)}, bf16[4,1,32,128]{3,1,2,0:T(2,128)(2,1)S(1)}, u32[]{:S(2)}, u32[]{:S(2)}) collective-permute-start(bf16[4,1,32,128]{3,1,2,0:T(2,128)(2,1)S(1)} %get-tuple-element.489), channel_id=1, source_target_pairs={{0,4},{4,8},{8,12},{1,5},{5,9},{9,13},{2,6},{6,10},{10,14},{3,7},{... | collective-permute-start | bytes 98312 | tf_op jit(solution)/shard_map/while/body/eval_jaxpr/ppermute | solution.py:18
  151.3 6.3 %collective-permute-start.6 = (bf16[4,18,1,128]{3,1,2,0:T(8,128)(2,1)S(1)}, bf16[4,18,1,128]{3,1,2,0:T(8,128)(2,1)S(1)}, u32[]{:S(2)}, u32[]{:S(2)}) collective-permute-start(bf16[4,18,1,128]{3,1,2,0:T(8,128)(2,1)S(1)} %get-tuple-element.490), channel_id=1, source_target_pairs={{1,0},{2,1},{3,2},{5,4},{6,5},{7,6},{9,8},{10,9},{11,10},{13,12},{... | collective-permute-start | bytes 55304 | tf_op jit(solution)/shard_map/while/body/eval_jaxpr/ppermute | solution.py:21
  152.6 6.5 %collective-permute-start.7 = (bf16[4,18,1,128]{3,1,2,0:T(8,128)(2,1)S(1)}, bf16[4,18,1,128]{3,1,2,0:T(8,128)(2,1)S(1)}, u32[]{:S(2)}, u32[]{:S(2)}) collective-permute-start(bf16[4,18,1,128]{3,1,2,0:T(8,128)(2,1)S(1)} %get-tuple-element.491), channel_id=1, source_target_pairs={{0,1},{1,2},{2,3},{4,5},{5,6},{6,7},{8,9},{9,10},{10,11},{12,13},{... | collective-permute-start | bytes 55304 | tf_op jit(solution)/shard_map/while/body/eval_jaxpr/ppermute | solution.py:18
  162.6 3.9 %collective-permute-start.8 = (bf16[4,16,32,128]{3,1,2,0:T(8,128)(2,1)S(1)}, bf16[4,16,32,128]{3,1,2,0:T(8,128)(2,1)}, u32[]{:S(2)}, u32[]{:S(2)}) collective-permute-start(bf16[4,16,32,128]{3,1,2,0:T(8,128)(2,1)S(1)} %slice_bitcast_fusion.7), channel_id=1, source_target_pairs={{16,0},{17,1},{18,2},{19,3},{20,4},{21,5},{22,6},{23,7},{24,8},{25... | collective-permute-start | bytes 1572872 | tf_op jit(solution)/shard_map/while/body/eval_jaxpr/ppermute | solution.py:29
  169.7 132.1 %copy-start.3 = (bf16[4,16,32,128]{3,2,1,0:T(8,128)(2,1)}, bf16[4,16,32,128]{3,2,1,0:T(8,128)(2,1)S(1)}, u32[]{:S(2)}) copy-start(bf16[4,16,32,128]{3,2,1,0:T(8,128)(2,1)S(1)} %scatter_fusion) | copy-start | bytes 1572868
  (12 other events, 21.8 us)
Sparse Core Ops, SparseCore 0:
  167.8 128.1 all-gather.2
